TPU v7x, 128 devices: a whole 4x4x4 slice. The times are simulated.
128 devices in a mesh: pipe: 2 (over core), dp: 16 (over y, x), tensor: 4 (over z).
Axes of the slice: x: 4, y: 4, z: 4, core: 2. Of those that a mesh axis runs over, the one named last changes fastest.
Arguments:
- weights: bfloat16 [2, 8192, 8192], P('pipe', 'tensor', 'dp'), may hold values from -0.0625 to 0.0625
- inputs: bfloat16 [2, 2, 32, 64, 8192], P('pipe', None, 'dp', None, 'tensor'), may hold values from -150 to 150
- cotangent: bfloat16 [2, 32, 64, 8192], P(None, 'dp', None, 'tensor'), may hold values from -6 to 6
- clip_norm: float32 [1], replicated, may hold values from 8192 to 12582912
- noise: bfloat16 [2, 8192, 8192], P('pipe', 'tensor', 'dp'), may hold values from -6 to 6
Outputs:
- grads: float32 [2, 8192, 8192], P('pipe', 'tensor', 'dp')
- clip_factors: float32 [2, 32], P(None, 'dp')
All inputs are finite; a program needn't handle non-finite values.
Results may differ from a plain program's by a relative error of at most 0.015.
Values may be sent and summed in bfloat16 or wider, within the bound.
No kernel may reach another device: no remote copies, remote signals or barrier semaphores. Data moves between devices by JAX's collectives and lax.ppermute only.
A program may use at most 128 MiB of HBM per device.

v0:
```python
import jax
import jax.numpy as jnp
from jax import lax
from jax.sharding import PartitionSpec as P


def swapped(value, axis):
    count = lax.axis_size(axis)
    return lax.ppermute(value, axis, [(source, count - 1 - source) for source in range(count)])


def to_column_blocks(values, group_count, column_part):
    micro_count, example_count, length_count, _ = values.shape
    token_count = example_count * length_count
    full = lax.all_gather(values, "tensor", axis=3, tiled=True)
    by_block = full.reshape(micro_count, token_count, group_count, column_part)
    moved = lax.all_to_all(by_block, "dp", split_axis=2, concat_axis=1, tiled=True)
    return moved.reshape(micro_count, group_count * token_count, column_part)


def grams(values):
    return lax.psum(
        jnp.einsum("...ld,...kd->...lk", values, values, preferred_element_type=jnp.float32),
        "tensor",
    )


def local(weights, inputs, cotangent, clip_norm, noise):
    section_index = lax.axis_index("pipe")
    group_count = lax.axis_size("dp")
    weight_block = weights[0]
    local_inputs = inputs[0]
    micro_count, example_count, length_count, width_part = local_inputs.shape
    token_count = example_count * length_count
    column_part = weight_block.shape[1]
    full_width = column_part * group_count
    is_last = section_index == 1
    gathered_inputs = lax.all_gather(local_inputs, "dp", axis=1, tiled=True)
    input_grams = grams(local_inputs)
    last_grams = grams(cotangent)
    last_blocks = to_column_blocks(cotangent, group_count, column_part)
    last_weights = jnp.where(is_last, weight_block, swapped(weight_block, "pipe"))
    own_blocks = lax.dynamic_index_in_dim(last_blocks, section_index, 0, keepdims=False)
    own_cotangent = lax.dynamic_index_in_dim(cotangent, section_index, 0, keepdims=False)
    terms = lax.dot_general(
        own_blocks, last_weights, (((1,), (1,)), ((), ())), preferred_element_type=jnp.float32
    ).astype(jnp.bfloat16)
    summed = lax.psum_scatter(terms, "dp", scatter_dimension=0, tiled=True).astype(jnp.float32)
    renewed = (
        (own_cotangent.reshape(token_count, width_part).astype(jnp.float32) + summed)
        .astype(jnp.bfloat16)
        .reshape(1, example_count, length_count, width_part)
    )
    own_first_grams = grams(renewed)
    other_first_grams = swapped(own_first_grams, "pipe")
    first_grams = jnp.where(
        is_last,
        jnp.concatenate([other_first_grams, own_first_grams], 0),
        jnp.concatenate([own_first_grams, other_first_grams], 0),
    )
    output_grams = jnp.where(is_last, last_grams, first_grams)
    section_terms = jnp.sum(input_grams * output_grams, axis=(2, 3))
    norm_square = lax.psum(section_terms, "pipe")
    bound = clip_norm[0]
    scale_terms = bound / jnp.maximum(jnp.sqrt(norm_square), bound)
    all_scales = lax.all_gather(scale_terms, "dp", axis=1, tiled=True)
    own_first_blocks = to_column_blocks(renewed, group_count, column_part)
    other_first_blocks = swapped(own_first_blocks, "pipe")
    first_blocks = jnp.where(
        is_last,
        jnp.concatenate([other_first_blocks, own_first_blocks], 0),
        jnp.concatenate([own_first_blocks, other_first_blocks], 0),
    )
    grad_blocks = jnp.where(is_last, last_blocks, first_blocks)
    clipped = (gathered_inputs.astype(jnp.float32) * all_scales[:, :, None, None]).astype(
        jnp.bfloat16
    )
    flat_inputs = clipped.reshape(micro_count * group_count * token_count, width_part)
    flat_grads = grad_blocks.reshape(micro_count * group_count * token_count, column_part)
    summed_grad = lax.dot_general(
        flat_inputs, flat_grads, (((0,), (0,)), ((), ())), preferred_element_type=jnp.float32
    )
    noise_weight = 1.5 / full_width
    per_example_sum = micro_count * group_count * example_count
    final_output = (
        summed_grad + noise_weight * bound * noise[0].astype(jnp.float32)
    ) / per_example_sum
    return (final_output[None], scale_terms)


def solution(mesh):
    in_specs = (
        P("pipe", "tensor", "dp"),
        P("pipe", None, "dp", None, "tensor"),
        P(None, "dp", None, "tensor"),
        P(),
        P("pipe", "tensor", "dp"),
    )
    out_specs = (P("pipe", "tensor", "dp"), P(None, "dp"))
    return jax.shard_map(local, mesh=mesh, in_specs=in_specs, out_specs=out_specs, check_vma=False)
```

profile of v0, /device:TPU:1, one launch (start us, length us, event | category | flops | bytes accessed | tf_op | source)
XLA Modules:
  0.0 456.7 jit_solution(14960222356371423096)
XLA Ops:
  7.2 0.0 all-gather.6.cloned.1.call-start
  7.2 0.7 all-gather.6.cloned.1.call-update
  7.9 53.2 %all-gather.6.cloned.1.call-done = bf16[2,2,64,8192]{3,2,1,0:T(8,128)(2,1)} async-done(((bf16[2,2,64,2048]{3,2,1,0:T(8,128)(2,1)}), bf16[2,2,64,8192]{3,2,1,0:T(8,128)(2,1)}) %all-gather.6.cloned.1.call-update) | async-done | bytes 4194320 | tf_op jit(solution)/shard_map/all_gather | solution.py:15
  61.1 4.0 copy.28
  65.2 4.4 copy.20
  69.6 0.0 copy-start.3
  69.6 6.7 %all-to-all-start = ((bf16[2,128,16,512]{3,1,0,2:T(8,128)(2,1)}), bf16[2,128,16,512]{3,1,0,2:T(8,128)(2,1)}, u32[]{:S(2)}, u32[]{:S(2)}) async-start(bf16[2,128,16,512]{3,1,0,2:T(8,128)(2,1)} %copy.20), calls=%async_computation | async-start | bytes 8388608 | tf_op jit(solution)/shard_map/all_to_all | solution.py:17
  76.3 0.0 reduce-scatter.2.cloned.1.call-start
  76.3 0.0 copy-done.3
  76.4 1.2 collective-permute-start
  77.6 60.9 %all-to-all-done = bf16[2,128,16,512]{3,1,0,2:T(8,128)(2,1)} async-done(((bf16[2,128,16,512]{3,1,0,2:T(8,128)(2,1)}), bf16[2,128,16,512]{3,1,0,2:T(8,128)(2,1)}, u32[]{:S(2)}, u32[]{:S(2)}) %all-to-all-start) | async-done | bytes 4194336 | tf_op jit(solution)/shard_map/all_to_all | solution.py:17
  138.4 2.6 copy.21
  141.1 0.0 collective-permute-done
  141.1 6.8 %convolution_convert_fusion = bf16[2048,2048]{1,0:T(8,128)(2,1)} fusion(bf16[2048,512]{1,0:T(8,128)(2,1)} %collective-permute-done, bf16[2,2048,512]{2,1,0:T(8,128)(2,1)S(1)} %bitcast.80, s32[]{:T(128)S(6)} %select_n.51, pred[]{:T(512)S(6)} %eq.3, bf16[1,2048,512]{2,1,0:T(8,128)(2,1)S(1)} %copy-done.3), kind=kOutput, calls=%fused_computation.2 | convolution fusion | flops 4300210176 | bytes 14680069 | tf_op jit(solution)/shard_map/dot_general | solution.py:45
  147.9 0.0 copy-start
  147.9 0.0 copy-start.2
  147.9 0.0 reduce-scatter.2.cloned.1.call-update
  147.9 0.0 all-gather.8.cloned.1.call-start
  147.9 1.1 copy-done
  149.1 83.8 %reduce-scatter.2.cloned.1.call-done = bf16[128,2048]{1,0:T(8,128)(2,1)} async-done(((bf16[2048,2048]{1,0:T(8,128)(2,1)}), bf16[128,2048]{1,0:T(8,128)(2,1)}) %reduce-scatter.2.cloned.1.call-update) | async-done | bytes 524304 | tf_op jit(solution)/shard_map/reduce_scatter | solution.py:48
  232.9 2.0 fusion.8
  234.9 0.0 all-gather.8.cloned.1.call-update
  234.9 0.0 all-reduce.3.cloned.1.call-start
  235.0 0.0 copy-done.2
  235.0 1.1 fusion.9
  236.0 1.1 fusion.16
  237.1 0.0 all-reduce.3.cloned.1.call-update
  237.1 0.0 all-gather.10.cloned.1.call-start
  237.2 0.5 all-gather.10.cloned.1.call-update
  237.7 29.0 %all-gather.8.cloned.1.call-done = bf16[1,2,64,8192]{3,2,1,0:T(8,128)(2,1)} async-done(((bf16[1,2,64,2048]{3,2,1,0:T(8,128)(2,1)}), bf16[1,2,64,8192]{3,2,1,0:T(8,128)(2,1)}) %all-gather.8.cloned.1.call-update) | async-done | bytes 2097168 | tf_op jit(solution)/shard_map/all_gather | solution.py:15
  266.8 2.4 copy.29
  269.2 0.0 copy-start.1
  269.2 2.5 copy.24
  271.7 6.5 %all-to-all-start.1 = ((bf16[1,128,16,512]{3,1,0,2:T(8,128)(2,1)}), bf16[1,128,16,512]{3,1,0,2:T(8,128)(2,1)S(1)}, u32[]{:S(2)}, u32[]{:S(2)}) async-start(bf16[1,128,16,512]{3,1,0,2:T(8,128)(2,1)} %copy.24), calls=%async_computation.2 | async-start | bytes 4194304 | tf_op jit(solution)/shard_map/all_to_all | solution.py:17
  278.2 0.0 copy-done.1
  278.2 0.3 convolution_bitcast_fusion
  278.5 13.0 %psum.30 = f32[1,2,64,64]{3,2,1,0:T(8,128)S(1)} all-reduce(f32[1,2,64,64]{3,2,1,0:T(8,128)S(1)} %convolution_bitcast_fusion), channel_id=1, replica_groups=mesh['pipe'=2,'dp'=16,'tensor'=4] {'tensor'}, use_global_device_ids=true, to_apply=%region_3.4 | all-reduce | flops 8192 | bytes 65536 | tf_op jit(solution)/shard_map/psum | solution.py:22
  291.5 3.9 collective-permute-start.1
  296.1 13.4 %all-reduce.3.cloned.1.call-done = (f32[2,2,64,64]{3,2,1,0:T(8,128)}, f32[2,2,64,64]{3,2,1,0:T(8,128)}) async-done(((f32[2,2,64,64]{3,2,1,0:T(8,128)}, f32[2,2,64,64]{3,2,1,0:T(8,128)}), (f32[2,2,64,64]{3,2,1,0:T(8,128)}, f32[2,2,64,64]{3,2,1,0:T(8,128)})) %all-reduce.3.cloned.1.call-update) | async-done | bytes 131088 | tf_op jit(solution)/shard_map/psum | solution.py:22
  309.5 0.0 collective-permute-done.1
  309.5 1.1 fusion.13
  310.6 4.6 %psum.31 = f32[2,2]{1,0:T(2,128)S(1)} all-reduce(f32[2,2]{1,0:T(2,128)S(1)} %fusion.13), channel_id=1, replica_groups=mesh['pipe'=2,'dp'=16,'tensor'=4] {'pipe'}, use_global_device_ids=true, to_apply=%region_5.6 | all-reduce | flops 4 | bytes 32 | tf_op jit(solution)/shard_map/psum | solution.py:63
  315.3 0.0 all-to-all-done.1
  315.3 0.3 collective-permute-start.2
  315.6 0.1 copy.22
  315.7 19.6 %all-gather.1 = f32[16,2,2]{2,1,0:T(2,128)S(1)} all-gather(f32[1,2,2]{2,1,0:T(2,128)S(1)} %bitcast.84), channel_id=1, replica_groups=mesh['pipe'=2,'dp'=16,'tensor'=4] {'dp'}, dimensions={0}, use_global_device_ids=true | all-gather | bytes 272 | tf_op jit(solution)/shard_map/all_gather | solution.py:66
  335.3 0.1 copy.27
  335.4 0.6 maximum_divide_fusion
  335.9 88.8 %all-gather.10.cloned.1.call-done = bf16[1,2,32,64,2048]{4,3,2,1,0:T(8,128)(2,1)} async-done(((bf16[1,2,2,64,2048]{4,3,2,1,0:T(8,128)(2,1)}), bf16[1,2,32,64,2048]{4,3,2,1,0:T(8,128)(2,1)}) %all-gather.10.cloned.1.call-update) | async-done | bytes 16777232 | tf_op jit(solution)/shard_map/all_gather | solution.py:38
  424.8 9.8 %fusion = bf16[2,32,64,2048]{3,2,1,0:T(8,128)(2,1)S(1)} fusion(bf16[1,2,32,64,2048]{4,3,2,1,0:T(8,128)(2,1)} %all-gather.10.cloned.1.call-done, f32[2,32]{1,0:T(2,128)S(1)} %bitcast.83), kind=kLoop, calls=%fused_computation.1 | loop fusion | flops 25165824 | bytes 33554688 | tf_op jit(solution)/shard_map/convert_element_type | solution.py:75
  434.6 0.0 collective-permute-done.2
  434.6 3.9 fusion.1
  438.5 11.6 %fusion.3 = f32[1,2048,512]{2,1,0:T(8,128)} fusion(bf16[1,2048,512]{2,1,0:T(8,128)(2,1)} %param.9, bf16[4096,2048]{1,0:T(8,128)(2,1)S(1)} %bitcast.71, bf16[4096,512]{1,0:T(8,128)(2,1)S(1)} %bitcast.79, f32[]{:T(128)S(6)} %mul_shard_map.3), kind=kOutput, calls=%fused_computation.7 | convolution fusion | flops 8594128896 | bytes 27262980 | tf_op jit(solution)/shard_map/dot_general | solution.py:80
  (2 shorter events, 0.0 us)
Async XLA Ops:
  7.2 54.0 %all-gather.6.cloned.1.call-start = ((), (), s32[]{:S(2)}) async-start(), calls=%async_computation.3 | async-start | bytes 5242880 | tf_op jit(solution)/shard_map/all_gather | solution.py:15
  69.6 6.8 %copy-start.3 = (bf16[1,2048,512]{2,1,0:T(8,128)(2,1)S(1)}, bf16[1,2048,512]{2,1,0:T(8,128)(2,1)}, u32[]{:S(2)}) copy-start(bf16[1,2048,512]{2,1,0:T(8,128)(2,1)} %param.5) | copy-start | bytes 6291460
  69.6 68.8 %all-to-all-start = ((bf16[2,128,16,512]{3,1,0,2:T(8,128)(2,1)}), bf16[2,128,16,512]{3,1,0,2:T(8,128)(2,1)}, u32[]{:S(2)}, u32[]{:S(2)}) async-start(bf16[2,128,16,512]{3,1,0,2:T(8,128)(2,1)} %copy.20), calls=%async_computation | async-start | bytes 8388608 | tf_op jit(solution)/shard_map/all_to_all | solution.py:17
  76.3 156.6 %reduce-scatter.2.cloned.1.call-start = ((), (), s32[]{:S(2)}) async-start(), calls=%async_computation.4 | async-start | bytes 8912896 | tf_op jit(solution)/shard_map/reduce_scatter | solution.py:48
  76.4 64.7 %collective-permute-start = (bf16[2048,512]{1,0:T(8,128)(2,1)S(1)}, bf16[2048,512]{1,0:T(8,128)(2,1)}, u32[]{:S(2)}, u32[]{:S(2)}) collective-permute-start(bf16[2048,512]{1,0:T(8,128)(2,1)S(1)} %bitcast.85), channel_id=1, source_target_pairs={{0,64},{64,0},{1,65},{65,1},{2,66},{66,2},{3,67},{67,3},{4,68},{68... | collective-permute-start | bytes 6291464 | tf_op jit(solution)/shard_map/ppermute | solution.py:9
  147.9 1.2 copy-start
  147.9 87.1 %copy-start.2 = (bf16[1,2,2,64,2048]{4,3,2,1,0:T(8,128)(2,1)S(1)}, bf16[1,2,2,64,2048]{4,3,2,1,0:T(8,128)(2,1)}, u32[]{:S(2)}) copy-start(bf16[1,2,2,64,2048]{4,3,2,1,0:T(8,128)(2,1)} %param.6) | copy-start | bytes 3145732
  147.9 118.9 %all-gather.8.cloned.1.call-start = ((), (), s32[]{:S(2)}) async-start(), calls=%async_computation.5 | async-start | bytes 2621440 | tf_op jit(solution)/shard_map/all_gather | solution.py:15
  234.9 74.6 %all-reduce.3.cloned.1.call-start = ((), (), s32[]{:S(2)}) async-start(), calls=%async_computation.7 | async-start | bytes 524288 | tf_op jit(solution)/shard_map/psum | solution.py:22
  237.1 187.6 %all-gather.10.cloned.1.call-start = ((), (), s32[]{:S(2)}) async-start(), calls=%async_computation.6 | async-start | bytes 17825792 | tf_op jit(solution)/shard_map/all_gather | solution.py:38
  269.2 9.0 %copy-start.1 = (bf16[128,2048]{1,0:T(8,128)(2,1)S(1)}, bf16[128,2048]{1,0:T(8,128)(2,1)}, u32[]{:S(2)}) copy-start(bf16[128,2048]{1,0:T(8,128)(2,1)} %fusion.8) | copy-start | bytes 1572868
  271.7 43.6 %all-to-all-start.1 = ((bf16[1,128,16,512]{3,1,0,2:T(8,128)(2,1)}), bf16[1,128,16,512]{3,1,0,2:T(8,128)(2,1)S(1)}, u32[]{:S(2)}, u32[]{:S(2)}) async-start(bf16[1,128,16,512]{3,1,0,2:T(8,128)(2,1)} %copy.24), calls=%async_computation.2 | async-start | bytes 4194304 | tf_op jit(solution)/shard_map/all_to_all | solution.py:17
  291.5 18.0 %collective-permute-start.1 = (f32[1,2,64,64]{3,2,1,0:T(8,128)S(1)}, f32[1,2,64,64]{3,2,1,0:T(8,128)S(1)}, u32[]{:S(2)}, u32[]{:S(2)}) collective-permute-start(f32[1,2,64,64]{3,2,1,0:T(8,128)S(1)} %psum.30), channel_id=1, source_target_pairs={{0,64},{64,0},{1,65},{65,1},{2,66},{66,2},{3,67},{67,3},{4,68},{68... | collective-permute-start | bytes 98312 | tf_op jit(solution)/shard_map/ppermute | solution.py:9
  315.3 119.3 %collective-permute-start.2 = (bf16[1,2048,512]{2,1,0:T(8,128)(2,1)S(1)}, bf16[1,2048,512]{2,1,0:T(8,128)(2,1)}, u32[]{:S(2)}, u32[]{:S(2)}) collective-permute-start(bf16[1,2048,512]{2,1,0:T(8,128)(2,1)S(1)} %bitcast.73), channel_id=1, source_target_pairs={{0,64},{64,0},{1,65},{65,1},{2,66},{66,2},{3,67},{67,3},{4,68},{68... | collective-permute-start | bytes 6291464 | tf_op jit(solution)/shard_map/ppermute | solution.py:9
Sparse Core Ops, SparseCore 0:
  9.6 51.4 all-gather.5
  148.0 84.8 reduce-scatter.1
  235.0 31.6 all-gather.7
  269.0 40.4 all-reduce.2
  311.5 113.2 all-gather.9
where the time goes:
time: 457 us
  waiting for transfers between devices  330 us (72%)
  blocking collectives  37.2 us (8%)
  matrix products  20.8 us (5%)
  starting transfers between devices  18.9 us (4%)
  local copies, waits for them, and re-layouts  17.4 us (4%)
  other arithmetic  17.4 us (4%)
  between operations  14.6 us (3%)
    all_gather x1, waiting for transfers between devices, local(): gathered_inputs = lax.all_gather(local_inputs, 'dp', axis=1, tiled=True)  88.8 us
    reduce_scatter x1, waiting for transfers between devices, local(): lax.psum_scatter(terms, 'dp', scatter_dimension=0, tiled=True)  83.8 us
    all_gather x2, waiting for transfers between devices, to_column_blocks(): full = lax.all_gather(values, 'tensor', axis=3, tiled=True)  82.3 us
    all_to_all x2, waiting for transfers between devices, to_column_blocks(): lax.all_to_all(by_block, 'dp', split_axis=2, concat_axis=1, tiled=True)  60.9 us
    all_gather x1, blocking collectives, local(): all_scales = lax.all_gather(scale_terms, 'dp', axis=1, tiled=True)  19.6 us
    psum x1, waiting for transfers between devices, grams(): lax.psum(jnp.einsum('...ld,...kd->...lk', values, values, preferred_eleme...  13.4 us
    all_to_all x2, starting transfers between devices, to_column_blocks(): lax.all_to_all(by_block, 'dp', split_axis=2, concat_axis=1, tiled=True)  13.2 us
    psum x1, blocking collectives, grams(): lax.psum(jnp.einsum('...ld,...kd->...lk', values, values, preferred_eleme...  13 us
  transfers between devices with their start and end apart: 10, of which 6 were waited for; matrix products, arithmetic and copies ran while one was open for 5% of the time, Pallas kernels for 0%

commit v1 on v0

--- a/solution.py
+++ b/solution.py
@@ -2,6 +2,27 @@
 import jax.numpy as jnp
 from jax import lax
 from jax.sharding import PartitionSpec as P
+
+
+def collect(x, axis, dim):
+    size, index, extent = (lax.axis_size(axis), lax.axis_index(axis), x.shape[dim])
+    right = [(i, (i + 1) % size) for i in range(size)]
+    downward = [(i, (i - 1) % size) for i in range(size)]
+    out = jnp.zeros((*x.shape[:dim], size * extent, *x.shape[dim + 1 :]), x.dtype)
+    out = lax.dynamic_update_slice_in_dim(out, x, index * extent, axis=dim)
+    from_left = from_right = x
+    half = size // 2
+    for lap in range(1, half + 1):
+        from_left = lax.ppermute(from_left, axis, right)
+        out = lax.dynamic_update_slice_in_dim(
+            out, from_left, (index - lap) % size * extent, axis=dim
+        )
+        if lap < size - half:
+            from_right = lax.ppermute(from_right, axis, downward)
+            out = lax.dynamic_update_slice_in_dim(
+                out, from_right, (index + lap) % size * extent, axis=dim
+            )
+    return out
 
 
 def swapped(value, axis):
@@ -35,7 +56,7 @@
     column_part = weight_block.shape[1]
     full_width = column_part * group_count
     is_last = section_index == 1
-    gathered_inputs = lax.all_gather(local_inputs, "dp", axis=1, tiled=True)
+    gathered_inputs = collect(local_inputs, "dp", 1)
     input_grams = grams(local_inputs)
     last_grams = grams(cotangent)
     last_blocks = to_column_blocks(cotangent, group_count, column_part)

time: 457 us -> 502 us (1.098); the launches traced: 457 us -> 496 us
  waiting for transfers between devices: 330 us -> 277 us
  starting transfers between devices: 18.9 us -> 71.3 us
  local copies, waits for them, and re-layouts: 17.4 us -> 57.7 us
    ppermute x0 -> x15, waiting for transfers between devices: none -> 95.7 us  [the longest x7 57.4 us: collect(): from_right = lax.ppermute(from_right, axis, downward)]
    all_gather x1 -> x0, waiting for transfers between devices: 88.8 us -> none  [local(): gathered_inputs = lax.all_gather(local_inputs, 'dp', axis=1, tiled=True)]
    dynamic_update_slice x0 -> x16, local copies, waits for them, and re-layouts: none -> 34.5 us  [the longest x8 17.2 us: collect(): lax.dynamic_update_slice_in_dim(out, from_left, (index - lap) % size * ex...]
    ppermute x0 -> x15, starting transfers between devices: none -> 34.1 us  [the longest x7 34 us: collect(): from_right = lax.ppermute(from_right, axis, downward)]
    all_gather x2, waiting for transfers between devices: 82.3 us -> 53.2 us  [to_column_blocks(): full = lax.all_gather(values, 'tensor', axis=3, tiled=True)]
    ppermute x3, starting transfers between devices: 5.45 us -> 24.3 us  [swapped(): lax.ppermute(value, axis, [(source, count - 1 - source) for source in ran...]
    reduce_scatter x1, waiting for transfers between devices: 83.8 us -> 66.2 us  [local(): lax.psum_scatter(terms, 'dp', scatter_dimension=0, tiled=True)]
    psum x1, waiting for transfers between devices: 13.4 us -> 0.01 us  [grams(): lax.psum(jnp.einsum('...ld,...kd->...lk', values, values, preferred_eleme...]
  transfers between devices with their start and end apart: 10 -> 24, of which waited for: 6 -> 10; matrix products, arithmetic and copies ran while one was open for 5% -> 13% of each run, Pallas kernels for 0% -> 0%
where the time goes in v1:
time: 502 us; the launch traced here: 496 us
  waiting for transfers between devices  277 us (55%)
  starting transfers between devices  71.3 us (14%)
  local copies, waits for them, and re-layouts  57.7 us (11%)
  blocking collectives  35.6 us (7%)
  matrix products  22.6 us (5%)
  other arithmetic  17.4 us (3%)
  between operations  14.6 us (3%)
    reduce_scatter x1, waiting for transfers between devices, local(): lax.psum_scatter(terms, 'dp', scatter_dimension=0, tiled=True)  66.2 us
    all_to_all x2, waiting for transfers between devices, to_column_blocks(): lax.all_to_all(by_block, 'dp', split_axis=2, concat_axis=1, tiled=True)  60.9 us
    ppermute x7, waiting for transfers between devices, collect(): from_right = lax.ppermute(from_right, axis, downward)  57.4 us
    all_gather x2, waiting for transfers between devices, to_column_blocks(): full = lax.all_gather(values, 'tensor', axis=3, tiled=True)  53.2 us
    ppermute x8, waiting for transfers between devices, collect(): from_left = lax.ppermute(from_left, axis, right)  38.3 us
    ppermute x7, starting transfers between devices, collect(): from_right = lax.ppermute(from_right, axis, downward)  34 us
    ppermute x3, starting transfers between devices, swapped(): lax.ppermute(value, axis, [(source, count - 1 - source) for source in ran...  24.3 us
    dynamic_update_slice x8, local copies, waits for them, and re-layouts, collect(): lax.dynamic_update_slice_in_dim(out, from_left, (index - lap) % size * ex...  17.2 us
  transfers between devices with their start and end apart: 24, of which 10 were waited for; matrix products, arithmetic and copies ran while one was open for 13% of the time, Pallas kernels for 0%

profile of v1, /device:TPU:1, one launch (start us, length us, event | category | flops | bytes accessed | tf_op | source)
XLA Modules:
  0.0 495.9 jit_solution(10785329222205550542)
XLA Ops:
  7.2 0.7 all-gather.4.cloned.1.call-update
  7.9 53.2 %all-gather.4.cloned.1.call-done = bf16[2,2,64,8192]{3,2,1,0:T(8,128)(2,1)} async-done(((bf16[2,2,64,2048]{3,2,1,0:T(8,128)(2,1)}), bf16[2,2,64,8192]{3,2,1,0:T(8,128)(2,1)}) %all-gather.4.cloned.1.call-update) | async-done | bytes 4194320 | tf_op jit(solution)/shard_map/all_gather | solution.py:36
  61.1 4.0 copy.28
  65.2 4.4 copy.20
  69.6 6.6 %all-to-all-start = ((bf16[2,128,16,512]{3,1,0,2:T(8,128)(2,1)}), bf16[2,128,16,512]{3,1,0,2:T(8,128)(2,1)}, u32[]{:S(2)}, u32[]{:S(2)}) async-start(bf16[2,128,16,512]{3,1,0,2:T(8,128)(2,1)} %copy.20), calls=%async_computation | async-start | bytes 8388608 | tf_op jit(solution)/shard_map/all_to_all | solution.py:38
  76.2 0.0 reduce-scatter.2.cloned.1.call-start
  76.2 1.2 collective-permute-start.15
  77.4 60.9 %all-to-all-done = bf16[2,128,16,512]{3,1,0,2:T(8,128)(2,1)} async-done(((bf16[2,128,16,512]{3,1,0,2:T(8,128)(2,1)}), bf16[2,128,16,512]{3,1,0,2:T(8,128)(2,1)}, u32[]{:S(2)}, u32[]{:S(2)}) %all-to-all-start) | async-done | bytes 4194336 | tf_op jit(solution)/shard_map/all_to_all | solution.py:38
  138.3 2.6 copy.21
  141.0 8.6 %convolution_convert_fusion = bf16[2048,2048]{1,0:T(8,128)(2,1)} fusion(bf16[2048,512]{1,0:T(8,128)(2,1)} %collective-permute-done.15, bf16[2,2048,512]{2,1,0:T(8,128)(2,1)S(1)} %bitcast.78, s32[]{:T(128)S(6)} %select_n.193, pred[]{:T(512)S(6)} %eq.19, bf16[1,2048,512]{2,1,0:T(8,128)(2,1)} %param.5), kind=kOutput, calls=%fused_computation.1 | convolution fusion | flops 4300210176 | bytes 14680069 | tf_op jit(solution)/shard_map/dot_general | solution.py:66
  149.6 0.0 all-gather.6.cloned.1.call-start
  149.6 0.1 collective-permute-start
  149.7 4.8 collective-permute-start.1
  154.5 31.4 %collective-permute-done = bf16[2,2,64,2048]{3,2,1,0:T(8,128)(2,1)} collective-permute-done((bf16[2,2,64,2048]{3,2,1,0:T(8,128)(2,1)S(1)}, bf16[2,2,64,2048]{3,2,1,0:T(8,128)(2,1)}, u32[]{:S(2)}, u32[]{:S(2)}) %collective-permute-start) | collective-permute-done | bytes 1048608 | tf_op jit(solution)/shard_map/ppermute | solution.py:16
  185.9 66.2 %reduce-scatter.2.cloned.1.call-done = bf16[128,2048]{1,0:T(8,128)(2,1)} async-done(((bf16[2048,2048]{1,0:T(8,128)(2,1)}), bf16[128,2048]{1,0:T(8,128)(2,1)}) %reduce-scatter.2.cloned.1.call-update) | async-done | bytes 524304 | tf_op jit(solution)/shard_map/reduce_scatter | solution.py:69
  252.0 2.0 fusion.7
  254.1 2.5 collective-permute-start.3
  256.6 20.8 %collective-permute-done.3 = bf16[2,2,64,2048]{3,2,1,0:T(8,128)(2,1)} collective-permute-done((bf16[2,2,64,2048]{3,2,1,0:T(8,128)(2,1)}, bf16[2,2,64,2048]{3,2,1,0:T(8,128)(2,1)}, u32[]{:S(2)}, u32[]{:S(2)}) %collective-permute-start.3) | collective-permute-done | bytes 1048608 | tf_op jit(solution)/shard_map/ppermute | solution.py:21
  277.4 5.5 %collective-permute-start.5 = (bf16[2,2,64,2048]{3,2,1,0:T(8,128)(2,1)}, bf16[2,2,64,2048]{3,2,1,0:T(8,128)(2,1)}, u32[]{:S(2)}, u32[]{:S(2)}) collective-permute-start(bf16[2,2,64,2048]{3,2,1,0:T(8,128)(2,1)} %collective-permute-done.3), channel_id=1, source_target_pairs={{0,60},{4,0},{8,4},{12,8},{16,12},{20,16},{24,20},{28,24},{32,28},... | collective-permute-start | bytes 3145736 | tf_op jit(solution)/shard_map/ppermute | solution.py:21
  282.9 1.0 copy-done.3
  283.9 19.0 %collective-permute-done.5 = bf16[2,2,64,2048]{3,2,1,0:T(8,128)(2,1)} collective-permute-done((bf16[2,2,64,2048]{3,2,1,0:T(8,128)(2,1)}, bf16[2,2,64,2048]{3,2,1,0:T(8,128)(2,1)}, u32[]{:S(2)}, u32[]{:S(2)}) %collective-permute-start.5) | collective-permute-done | bytes 1048608 | tf_op jit(solution)/shard_map/ppermute | solution.py:21
  302.8 5.5 %collective-permute-start.7 = (bf16[2,2,64,2048]{3,2,1,0:T(8,128)(2,1)}, bf16[2,2,64,2048]{3,2,1,0:T(8,128)(2,1)}, u32[]{:S(2)}, u32[]{:S(2)}) collective-permute-start(bf16[2,2,64,2048]{3,2,1,0:T(8,128)(2,1)} %collective-permute-done.5), channel_id=1, source_target_pairs={{0,60},{4,0},{8,4},{12,8},{16,12},{20,16},{24,20},{28,24},{32,28},... | collective-permute-start | bytes 3145736 | tf_op jit(solution)/shard_map/ppermute | solution.py:21
  308.4 0.5 collective-permute-done.6
  308.8 1.1 fusion.13
  309.9 1.1 fusion.15
  311.0 16.4 %collective-permute-done.7 = bf16[2,2,64,2048]{3,2,1,0:T(8,128)(2,1)} collective-permute-done((bf16[2,2,64,2048]{3,2,1,0:T(8,128)(2,1)}, bf16[2,2,64,2048]{3,2,1,0:T(8,128)(2,1)}, u32[]{:S(2)}, u32[]{:S(2)}) %collective-permute-start.7) | collective-permute-done | bytes 1048608 | tf_op jit(solution)/shard_map/ppermute | solution.py:21
  327.5 5.5 %collective-permute-start.9 = (bf16[2,2,64,2048]{3,2,1,0:T(8,128)(2,1)}, bf16[2,2,64,2048]{3,2,1,0:T(8,128)(2,1)}, u32[]{:S(2)}, u32[]{:S(2)}) collective-permute-start(bf16[2,2,64,2048]{3,2,1,0:T(8,128)(2,1)} %collective-permute-done.7), channel_id=1, source_target_pairs={{0,60},{4,0},{8,4},{12,8},{16,12},{20,16},{24,20},{28,24},{32,28},... | collective-permute-start | bytes 3145736 | tf_op jit(solution)/shard_map/ppermute | solution.py:21
  333.0 6.0 %broadcast_in_dim.7 = bf16[2,32,64,2048]{3,2,1,0:T(8,128)(2,1)} broadcast(bf16[]{:T(256)} %constant.105.clone.1), dimensions={} | broadcast | bytes 16777218 | tf_op jit(solution)/shard_map/broadcast_in_dim | solution.py:11
  338.9 1.1 constant_dynamic-update-slice_fusion.15
  340.7 2.3 constant_dynamic-update-slice_fusion.14
  343.1 2.3 constant_dynamic-update-slice_fusion.13
  345.4 2.3 constant_dynamic-update-slice_fusion.12
  347.7 2.4 constant_dynamic-update-slice_fusion.11
  350.0 1.2 collective-permute-done.9
  351.2 5.5 %collective-permute-start.11 = (bf16[2,2,64,2048]{3,2,1,0:T(8,128)(2,1)}, bf16[2,2,64,2048]{3,2,1,0:T(8,128)(2,1)}, u32[]{:S(2)}, u32[]{:S(2)}) collective-permute-start(bf16[2,2,64,2048]{3,2,1,0:T(8,128)(2,1)} %collective-permute-done.9), channel_id=1, source_target_pairs={{0,60},{4,0},{8,4},{12,8},{16,12},{20,16},{24,20},{28,24},{32,28},... | collective-permute-start | bytes 3145736 | tf_op jit(solution)/shard_map/ppermute | solution.py:21
  356.7 1.0 constant_dynamic-update-slice_fusion.10
  357.8 2.3 constant_dynamic-update-slice_fusion.9
  360.1 6.4 %collective-permute-done.10 = bf16[2,2,64,2048]{3,2,1,0:T(8,128)(2,1)} collective-permute-done((bf16[2,2,64,2048]{3,2,1,0:T(8,128)(2,1)}, bf16[2,2,64,2048]{3,2,1,0:T(8,128)(2,1)}, u32[]{:S(2)}, u32[]{:S(2)}) %collective-permute-start.10) | collective-permute-done | bytes 1048608 | tf_op jit(solution)/shard_map/ppermute | solution.py:16
  366.5 2.3 constant_dynamic-update-slice_fusion.8
  368.8 2.3 constant_dynamic-update-slice_fusion.7
  371.1 2.4 copy.29
  373.5 2.5 copy.24
  376.0 6.2 %all-to-all-start.1 = ((bf16[1,128,16,512]{3,1,0,2:T(8,128)(2,1)}), bf16[1,128,16,512]{3,1,0,2:T(8,128)(2,1)S(1)}, u32[]{:S(2)}, u32[]{:S(2)}) async-start(bf16[1,128,16,512]{3,1,0,2:T(8,128)(2,1)} %copy.24), calls=%async_computation.2 | async-start | bytes 4194304 | tf_op jit(solution)/shard_map/all_to_all | solution.py:38
  382.2 2.3 constant_dynamic-update-slice_fusion.6
  384.6 4.7 collective-permute-start.13
  389.3 2.3 constant_dynamic-update-slice_fusion.5
  391.6 2.3 constant_dynamic-update-slice_fusion.4
  393.9 2.3 constant_dynamic-update-slice_fusion.3
  396.2 2.3 constant_dynamic-update-slice_fusion.2
  398.5 0.3 convolution_bitcast_fusion
  398.8 14.9 %psum.30 = f32[1,2,64,64]{3,2,1,0:T(8,128)S(1)} all-reduce(f32[1,2,64,64]{3,2,1,0:T(8,128)S(1)} %convolution_bitcast_fusion), channel_id=1, replica_groups=mesh['pipe'=2,'dp'=16,'tensor'=4] {'tensor'}, use_global_device_ids=true, to_apply=%region_3.4 | all-reduce | flops 8192 | bytes 65536 | tf_op jit(solution)/shard_map/psum | solution.py:43
  413.7 22.7 %collective-permute-start.16 = (f32[1,2,64,64]{3,2,1,0:T(8,128)S(1)}, f32[1,2,64,64]{3,2,1,0:T(8,128)S(1)}, u32[]{:S(2)}, u32[]{:S(2)}) collective-permute-start(f32[1,2,64,64]{3,2,1,0:T(8,128)S(1)} %psum.30), channel_id=1, source_target_pairs={{0,64},{64,0},{1,65},{65,1},{2,66},{66,2},{3,67},{67,3},{4,68},{68... | collective-permute-start | bytes 98312 | tf_op jit(solution)/shard_map/ppermute | solution.py:30
  436.4 2.3 constant_dynamic-update-slice_fusion.1
  438.7 1.1 fusion.10
  439.8 2.4 constant_dynamic-update-slice_fusion
  442.2 5.9 %psum.31 = f32[2,2]{1,0:T(2,128)S(1)} all-reduce(f32[2,2]{1,0:T(2,128)S(1)} %fusion.10), channel_id=1, replica_groups=mesh['pipe'=2,'dp'=16,'tensor'=4] {'pipe'}, use_global_device_ids=true, to_apply=%region_5.6 | all-reduce | flops 4 | bytes 32 | tf_op jit(solution)/shard_map/psum | solution.py:84
  448.1 0.3 collective-permute-start.17
  448.4 0.1 copy.22
  448.5 14.9 %all-gather = f32[16,2,2]{2,1,0:T(2,128)S(1)} all-gather(f32[1,2,2]{2,1,0:T(2,128)S(1)} %bitcast.84), channel_id=1, replica_groups=mesh['pipe'=2,'dp'=16,'tensor'=4] {'dp'}, dimensions={0}, use_global_device_ids=true | all-gather | bytes 272 | tf_op jit(solution)/shard_map/all_gather | solution.py:87
  463.4 0.1 copy.27
  463.4 0.6 maximum_divide_fusion
  464.0 9.8 %multiply_convert_fusion = bf16[2,32,64,2048]{3,2,1,0:T(8,128)(2,1)S(1)} fusion(bf16[2,32,64,2048]{3,2,1,0:T(8,128)(2,1)} %constant_dynamic-update-slice_fusion, f32[2,32]{1,0:T(2,128)S(1)} %bitcast.83), kind=kLoop, calls=%fused_computation | loop fusion | flops 25165824 | bytes 33554688 | tf_op jit(solution)/shard_map/convert_element_type | solution.py:96
  473.8 3.9 fusion
  477.8 11.6 %fusion.2 = f32[1,2048,512]{2,1,0:T(8,128)} fusion(bf16[1,2048,512]{2,1,0:T(8,128)(2,1)} %param.9, bf16[4096,2048]{1,0:T(8,128)(2,1)S(1)} %bitcast.69, bf16[4096,512]{1,0:T(8,128)(2,1)S(1)} %bitcast.77, f32[]{:T(128)S(6)} %mul_shard_map.3), kind=kOutput, calls=%fused_computation.6 | convolution fusion | flops 8594128896 | bytes 27262980 | tf_op jit(solution)/shard_map/dot_general | solution.py:101
  (39 shorter events, 0.3 us)
Async XLA Ops:
  7.2 69.1 %copy-start.5 = (bf16[1,2048,512]{2,1,0:T(8,128)(2,1)S(1)}, bf16[1,2048,512]{2,1,0:T(8,128)(2,1)}, u32[]{:S(2)}) copy-start(bf16[1,2048,512]{2,1,0:T(8,128)(2,1)} %param.5) | copy-start | bytes 6291460
  7.2 54.0 %all-gather.4.cloned.1.call-start = ((), (), s32[]{:S(2)}) async-start(), calls=%async_computation.3 | async-start | bytes 5242880 | tf_op jit(solution)/shard_map/all_gather | solution.py:36
  69.6 68.7 %all-to-all-start = ((bf16[2,128,16,512]{3,1,0,2:T(8,128)(2,1)}), bf16[2,128,16,512]{3,1,0,2:T(8,128)(2,1)}, u32[]{:S(2)}, u32[]{:S(2)}) async-start(bf16[2,128,16,512]{3,1,0,2:T(8,128)(2,1)} %copy.20), calls=%async_computation | async-start | bytes 8388608 | tf_op jit(solution)/shard_map/all_to_all | solution.py:38
  76.2 175.9 %reduce-scatter.2.cloned.1.call-start = ((), (), s32[]{:S(2)}) async-start(), calls=%async_computation.4 | async-start | bytes 8912896 | tf_op jit(solution)/shard_map/reduce_scatter | solution.py:69
  76.2 64.7 %collective-permute-start.15 = (bf16[2048,512]{1,0:T(8,128)(2,1)S(1)}, bf16[2048,512]{1,0:T(8,128)(2,1)}, u32[]{:S(2)}, u32[]{:S(2)}) collective-permute-start(bf16[2048,512]{1,0:T(8,128)(2,1)S(1)} %bitcast.85), channel_id=1, source_target_pairs={{0,64},{64,0},{1,65},{65,1},{2,66},{66,2},{3,67},{67,3},{4,68},{68... | collective-permute-start | bytes 6291464 | tf_op jit(solution)/shard_map/ppermute | solution.py:30
  140.9 8.7 %copy-start.2 = (bf16[1,2,2,64,2048]{4,3,2,1,0:T(8,128)(2,1)S(1)}, bf16[1,2,2,64,2048]{4,3,2,1,0:T(8,128)(2,1)}, u32[]{:S(2)}) copy-start(bf16[1,2,2,64,2048]{4,3,2,1,0:T(8,128)(2,1)} %param.6) | copy-start | bytes 3145732
  141.0 44.9 %copy-start = (bf16[2,2,64,2048]{3,2,1,0:T(8,128)(2,1)S(1)}, bf16[2,2,64,2048]{3,2,1,0:T(8,128)(2,1)}, u32[]{:S(2)}) copy-start(bf16[2,2,64,2048]{3,2,1,0:T(8,128)(2,1)} %param.7) | copy-start | bytes 3145732
  149.6 221.6 %all-gather.6.cloned.1.call-start = ((), (), s32[]{:S(2)}) async-start(), calls=%async_computation.5 | async-start | bytes 2621440 | tf_op jit(solution)/shard_map/all_gather | solution.py:36
  149.6 36.2 %collective-permute-start = (bf16[2,2,64,2048]{3,2,1,0:T(8,128)(2,1)S(1)}, bf16[2,2,64,2048]{3,2,1,0:T(8,128)(2,1)}, u32[]{:S(2)}, u32[]{:S(2)}) collective-permute-start(bf16[2,2,64,2048]{3,2,1,0:T(8,128)(2,1)S(1)} %bitcast.80), channel_id=1, source_target_pairs={{0,4},{4,8},{8,12},{12,16},{16,20},{20,24},{24,28},{28,32},{32,36}... | collective-permute-start | bytes 3145736 | tf_op jit(solution)/shard_map/ppermute | solution.py:16
  149.7 104.4 %collective-permute-start.1 = (bf16[2,2,64,2048]{3,2,1,0:T(8,128)(2,1)S(1)}, bf16[2,2,64,2048]{3,2,1,0:T(8,128)(2,1)}, u32[]{:S(2)}, u32[]{:S(2)}) collective-permute-start(bf16[2,2,64,2048]{3,2,1,0:T(8,128)(2,1)S(1)} %bitcast.81), channel_id=1, source_target_pairs={{0,60},{4,0},{8,4},{12,8},{16,12},{20,16},{24,20},{28,24},{32,28},... | collective-permute-start | bytes 3145736 | tf_op jit(solution)/shard_map/ppermute | solution.py:21
  185.8 70.8 %collective-permute-start.2 = (bf16[2,2,64,2048]{3,2,1,0:T(8,128)(2,1)}, bf16[2,2,64,2048]{3,2,1,0:T(8,128)(2,1)}, u32[]{:S(2)}, u32[]{:S(2)}) collective-permute-start(bf16[2,2,64,2048]{3,2,1,0:T(8,128)(2,1)} %collective-permute-done), channel_id=1, source_target_pairs={{0,4},{4,8},{8,12},{12,16},{16,20},{20,24},{24,28},{28,32},{32,36}... | collective-permute-start | bytes 3145736 | tf_op jit(solution)/shard_map/ppermute | solution.py:16
  254.0 184.7 %all-reduce.3.cloned.1.call-start = ((), (), s32[]{:S(2)}) async-start(), calls=%async_computation.6 | async-start | bytes 524288 | tf_op jit(solution)/shard_map/psum | solution.py:43
  254.1 23.3 %collective-permute-start.3 = (bf16[2,2,64,2048]{3,2,1,0:T(8,128)(2,1)}, bf16[2,2,64,2048]{3,2,1,0:T(8,128)(2,1)}, u32[]{:S(2)}, u32[]{:S(2)}) collective-permute-start(bf16[2,2,64,2048]{3,2,1,0:T(8,128)(2,1)} %collective-permute-done.1), channel_id=1, source_target_pairs={{0,60},{4,0},{8,4},{12,8},{16,12},{20,16},{24,20},{28,24},{32,28},... | collective-permute-start | bytes 3145736 | tf_op jit(solution)/shard_map/ppermute | solution.py:21
  256.6 26.3 %collective-permute-start.4 = (bf16[2,2,64,2048]{3,2,1,0:T(8,128)(2,1)}, bf16[2,2,64,2048]{3,2,1,0:T(8,128)(2,1)S(1)}, u32[]{:S(2)}, u32[]{:S(2)}) collective-permute-start(bf16[2,2,64,2048]{3,2,1,0:T(8,128)(2,1)} %collective-permute-done.2), channel_id=1, source_target_pairs={{0,4},{4,8},{8,12},{12,16},{16,20},{20,24},{24,28},{28,32},{32,36}... | collective-permute-start | bytes 3145736 | tf_op jit(solution)/shard_map/ppermute | solution.py:16
  277.4 25.5 %collective-permute-start.5 = (bf16[2,2,64,2048]{3,2,1,0:T(8,128)(2,1)}, bf16[2,2,64,2048]{3,2,1,0:T(8,128)(2,1)}, u32[]{:S(2)}, u32[]{:S(2)}) collective-permute-start(bf16[2,2,64,2048]{3,2,1,0:T(8,128)(2,1)} %collective-permute-done.3), channel_id=1, source_target_pairs={{0,60},{4,0},{8,4},{12,8},{16,12},{20,16},{24,20},{28,24},{32,28},... | collective-permute-start | bytes 3145736 | tf_op jit(solution)/shard_map/ppermute | solution.py:21
  282.9 1.0 copy-start.3
  283.9 25.0 %collective-permute-start.6 = (bf16[2,2,64,2048]{3,2,1,0:T(8,128)(2,1)S(1)}, bf16[2,2,64,2048]{3,2,1,0:T(8,128)(2,1)}, u32[]{:S(2)}, u32[]{:S(2)}) collective-permute-start(bf16[2,2,64,2048]{3,2,1,0:T(8,128)(2,1)S(1)} %collective-permute-done.4), channel_id=1, source_target_pairs={{0,4},{4,8},{8,12},{12,16},{16,20},{20,24},{24,28},{28,32},{32,36}... | collective-permute-start | bytes 3145736 | tf_op jit(solution)/shard_map/ppermute | solution.py:16
  302.8 24.6 %collective-permute-start.7 = (bf16[2,2,64,2048]{3,2,1,0:T(8,128)(2,1)}, bf16[2,2,64,2048]{3,2,1,0:T(8,128)(2,1)}, u32[]{:S(2)}, u32[]{:S(2)}) collective-permute-start(bf16[2,2,64,2048]{3,2,1,0:T(8,128)(2,1)} %collective-permute-done.5), channel_id=1, source_target_pairs={{0,60},{4,0},{8,4},{12,8},{16,12},{20,16},{24,20},{28,24},{32,28},... | collective-permute-start | bytes 3145736 | tf_op jit(solution)/shard_map/ppermute | solution.py:21
  308.8 34.2 %collective-permute-start.8 = (bf16[2,2,64,2048]{3,2,1,0:T(8,128)(2,1)}, bf16[2,2,64,2048]{3,2,1,0:T(8,128)(2,1)}, u32[]{:S(2)}, u32[]{:S(2)}) collective-permute-start(bf16[2,2,64,2048]{3,2,1,0:T(8,128)(2,1)} %collective-permute-done.6), channel_id=1, source_target_pairs={{0,4},{4,8},{8,12},{12,16},{16,20},{20,24},{24,28},{28,32},{32,36}... | collective-permute-start | bytes 3145736 | tf_op jit(solution)/shard_map/ppermute | solution.py:16
  311.0 45.8 %copy-start.4 = (bf16[2,2,64,2048]{3,2,1,0:T(8,128)(2,1)S(1)}, bf16[2,2,64,2048]{3,2,1,0:T(8,128)(2,1)}, u32[]{:S(2)}) copy-start(bf16[2,2,64,2048]{3,2,1,0:T(8,128)(2,1)} %copy-done.3) | copy-start | bytes 3145732
  327.5 23.8 %collective-permute-start.9 = (bf16[2,2,64,2048]{3,2,1,0:T(8,128)(2,1)}, bf16[2,2,64,2048]{3,2,1,0:T(8,128)(2,1)}, u32[]{:S(2)}, u32[]{:S(2)}) collective-permute-start(bf16[2,2,64,2048]{3,2,1,0:T(8,128)(2,1)} %collective-permute-done.7), channel_id=1, source_target_pairs={{0,60},{4,0},{8,4},{12,8},{16,12},{20,16},{24,20},{28,24},{32,28},... | collective-permute-start | bytes 3145736 | tf_op jit(solution)/shard_map/ppermute | solution.py:21
  343.0 23.5 %collective-permute-start.10 = (bf16[2,2,64,2048]{3,2,1,0:T(8,128)(2,1)}, bf16[2,2,64,2048]{3,2,1,0:T(8,128)(2,1)}, u32[]{:S(2)}, u32[]{:S(2)}) collective-permute-start(bf16[2,2,64,2048]{3,2,1,0:T(8,128)(2,1)} %collective-permute-done.8), channel_id=1, source_target_pairs={{0,4},{4,8},{8,12},{12,16},{16,20},{20,24},{24,28},{28,32},{32,36}... | collective-permute-start | bytes 3145736 | tf_op jit(solution)/shard_map/ppermute | solution.py:16
  347.7 50.8 %copy-start.1 = (bf16[128,2048]{1,0:T(8,128)(2,1)S(1)}, bf16[128,2048]{1,0:T(8,128)(2,1)}, u32[]{:S(2)}) copy-start(bf16[128,2048]{1,0:T(8,128)(2,1)} %fusion.7) | copy-start | bytes 1572868
  351.2 33.4 %collective-permute-start.11 = (bf16[2,2,64,2048]{3,2,1,0:T(8,128)(2,1)}, bf16[2,2,64,2048]{3,2,1,0:T(8,128)(2,1)}, u32[]{:S(2)}, u32[]{:S(2)}) collective-permute-start(bf16[2,2,64,2048]{3,2,1,0:T(8,128)(2,1)} %collective-permute-done.9), channel_id=1, source_target_pairs={{0,60},{4,0},{8,4},{12,8},{16,12},{20,16},{24,20},{28,24},{32,28},... | collective-permute-start | bytes 3145736 | tf_op jit(solution)/shard_map/ppermute | solution.py:21
  366.5 27.4 %collective-permute-start.12 = (bf16[2,2,64,2048]{3,2,1,0:T(8,128)(2,1)}, bf16[2,2,64,2048]{3,2,1,0:T(8,128)(2,1)}, u32[]{:S(2)}, u32[]{:S(2)}) collective-permute-start(bf16[2,2,64,2048]{3,2,1,0:T(8,128)(2,1)} %collective-permute-done.10), channel_id=1, source_target_pairs={{0,4},{4,8},{8,12},{12,16},{16,20},{20,24},{24,28},{28,32},{32,36}... | collective-permute-start | bytes 3145736 | tf_op jit(solution)/shard_map/ppermute | solution.py:16
  376.0 72.0 %all-to-all-start.1 = ((bf16[1,128,16,512]{3,1,0,2:T(8,128)(2,1)}), bf16[1,128,16,512]{3,1,0,2:T(8,128)(2,1)S(1)}, u32[]{:S(2)}, u32[]{:S(2)}) async-start(bf16[1,128,16,512]{3,1,0,2:T(8,128)(2,1)} %copy.24), calls=%async_computation.2 | async-start | bytes 4194304 | tf_op jit(solution)/shard_map/all_to_all | solution.py:38
  384.6 51.8 %collective-permute-start.13 = (bf16[2,2,64,2048]{3,2,1,0:T(8,128)(2,1)}, bf16[2,2,64,2048]{3,2,1,0:T(8,128)(2,1)}, u32[]{:S(2)}, u32[]{:S(2)}) collective-permute-start(bf16[2,2,64,2048]{3,2,1,0:T(8,128)(2,1)} %collective-permute-done.11), channel_id=1, source_target_pairs={{0,60},{4,0},{8,4},{12,8},{16,12},{20,16},{24,20},{28,24},{32,28},... | collective-permute-start | bytes 3145736 | tf_op jit(solution)/shard_map/ppermute | solution.py:21
  393.9 45.9 %collective-permute-start.14 = (bf16[2,2,64,2048]{3,2,1,0:T(8,128)(2,1)}, bf16[2,2,64,2048]{3,2,1,0:T(8,128)(2,1)}, u32[]{:S(2)}, u32[]{:S(2)}) collective-permute-start(bf16[2,2,64,2048]{3,2,1,0:T(8,128)(2,1)} %collective-permute-done.12), channel_id=1, source_target_pairs={{0,4},{4,8},{8,12},{12,16},{16,20},{20,24},{24,28},{28,32},{32,36}... | collective-permute-start | bytes 3145736 | tf_op jit(solution)/shard_map/ppermute | solution.py:16
  413.7 25.1 %collective-permute-start.16 = (f32[1,2,64,64]{3,2,1,0:T(8,128)S(1)}, f32[1,2,64,64]{3,2,1,0:T(8,128)S(1)}, u32[]{:S(2)}, u32[]{:S(2)}) collective-permute-start(f32[1,2,64,64]{3,2,1,0:T(8,128)S(1)} %psum.30), channel_id=1, source_target_pairs={{0,64},{64,0},{1,65},{65,1},{2,66},{66,2},{3,67},{67,3},{4,68},{68... | collective-permute-start | bytes 98312 | tf_op jit(solution)/shard_map/ppermute | solution.py:30
  448.1 25.8 %collective-permute-start.17 = (bf16[1,2048,512]{2,1,0:T(8,128)(2,1)S(1)}, bf16[1,2048,512]{2,1,0:T(8,128)(2,1)}, u32[]{:S(2)}, u32[]{:S(2)}) collective-permute-start(bf16[1,2048,512]{2,1,0:T(8,128)(2,1)S(1)} %bitcast.71), channel_id=1, source_target_pairs={{0,64},{64,0},{1,65},{65,1},{2,66},{66,2},{3,67},{67,3},{4,68},{68... | collective-permute-start | bytes 6291464 | tf_op jit(solution)/shard_map/ppermute | solution.py:30
Sparse Core Ops, SparseCore 0:
  9.6 51.4 all-gather.3
  149.7 102.3 reduce-scatter.1
  254.2 31.6 all-gather.5
  311.1 44.6 all-reduce.2
